TPU v7x, 32 devices: a whole 2x2x4 slice. The times are simulated.
32 devices in a mesh: real: 2 (over x), los: 8 (over z, y), sky: 2 (over core).
Axes of the slice: x: 2, y: 2, z: 4, core: 2. Of those that a mesh axis runs over, the one named last changes fastest.
Arguments:
- density: float32 [16, 2048, 2048], P(('real', 'los'), 'sky'), parts along dimension 0, may hold values from -6 to 8
- lens_weight: float32 [16], P(('real', 'los')), parts along dimension 0, may hold values from 0.05 to 0.4
- plane_count: int32 [16], P(('real', 'los')), parts along dimension 0, may hold values from 0 to 1
- ray_state: float32 [16, 12, 32, 2048], P(('real', 'los'), None, 'sky'), parts along dimension 0, may hold values from -6 to 6
Outputs:
- ray_out: float32 [16, 12, 32, 2048], P(('real', 'los'), None, 'sky'), parts along dimension 0
There are 2 independent parts, one for each index of `real`. A program takes and returns all parts, laid end to end along the dimension named above; each array names one. Nothing has to cross between parts.
All inputs are finite; a program needn't handle non-finite values.
Results may differ from a plain program's by a relative error of at most 0.00012.
Values sent between devices are 32-bit elements; how exact they have to be, the bound alone decides.
No kernel may reach another device: no remote copies, remote signals or barrier semaphores. Data moves between devices by JAX's collectives and lax.ppermute only.
A program may use at most 128 MiB of HBM per device.

v0:
```python
import math
import jax
import jax.numpy as jnp
from jax import lax
from jax.sharding import PartitionSpec as P

HOPS = 4
two_pi = 2.0 * math.pi
highest = lax.Precision.HIGHEST
first_radix = 16


def shifted(block, axis, distance):
    devices = range(lax.axis_size(axis))
    route = [((i - distance) % len(devices), i) for i in devices]
    return lax.ppermute(block, axis, route)


def lens_step(ray_tile, fields):
    disp_x = ray_tile[..., 0, :, :]
    disp_y = ray_tile[..., 1, :, :]
    tilt_x = ray_tile[..., 2, :, :]
    tilt_y = ray_tile[..., 3, :, :]
    jac_xx = ray_tile[..., 4, :, :]
    jac_xy = ray_tile[..., 5, :, :]
    jac_yx = ray_tile[..., 6, :, :]
    jac_yy = ray_tile[..., 7, :, :]
    rate_xx = ray_tile[..., 8, :, :]
    rate_xy = ray_tile[..., 9, :, :]
    rate_yx = ray_tile[..., 10, :, :]
    rate_yy = ray_tile[..., 11, :, :]
    bend_x = fields[..., 0, :, :]
    bend_y = fields[..., 1, :, :]
    hess_xx = fields[..., 2, :, :]
    hess_yy = fields[..., 3, :, :]
    hess_xy = fields[..., 4, :, :]
    push_x = bend_x + hess_xx * disp_x + hess_xy * disp_y
    push_y = bend_y + hess_xy * disp_x + hess_yy * disp_y
    new_tilt_x = tilt_x - push_x
    new_tilt_y = tilt_y - push_y
    new_disp_x = disp_x + new_tilt_x
    new_disp_y = disp_y + new_tilt_y
    new_rate_xx = rate_xx - (hess_xx * jac_xx + hess_xy * jac_yx)
    new_rate_xy = rate_xy - (hess_xx * jac_xy + hess_xy * jac_yy)
    new_rate_yx = rate_yx - (hess_xy * jac_xx + hess_yy * jac_yx)
    new_rate_yy = rate_yy - (hess_xy * jac_xy + hess_yy * jac_yy)
    new_jac_xx = jac_xx + new_rate_xx
    new_jac_xy = jac_xy + new_rate_xy
    new_jac_yx = jac_yx + new_rate_yx
    new_jac_yy = jac_yy + new_rate_yy
    return jnp.stack(
        [
            new_disp_x,
            new_disp_y,
            new_tilt_x,
            new_tilt_y,
            new_jac_xx,
            new_jac_xy,
            new_jac_yx,
            new_jac_yy,
            new_rate_xx,
            new_rate_xy,
            new_rate_yx,
            new_rate_yy,
        ],
        axis=-3,
    )


def phase_table(left_idx, right_idx, modulus, orient):
    product = left_idx[:, None] * right_idx[None, :] % modulus
    angle = orient * two_pi / modulus * product.astype(jnp.float32)
    return (jnp.cos(angle), jnp.sin(angle))


def mixed(form, left_op, right_op):
    return jnp.einsum(
        form, left_op, right_op, precision=highest, preferred_element_type=jnp.float32
    )


def complex_product(form, real_in, imag_in, table_re, table_im):
    if imag_in is None:
        return (mixed(form, real_in, table_re), mixed(form, real_in, table_im))
    out_re = mixed(form, real_in, table_re) - mixed(form, imag_in, table_im)
    out_im = mixed(form, real_in, table_im) + mixed(form, imag_in, table_re)
    return (out_re, out_im)


def first_factor_of(length):
    factor_one = 1
    while factor_one * factor_one < length and length % (factor_one * 2) == 0:
        factor_one = factor_one * 2
    return factor_one


def rows_forward(cells, k_count, m_count):
    row_count, length = cells.shape
    second = length // first_radix
    shaped = cells.reshape(row_count, first_radix, second)
    v_idx = jnp.arange(first_radix, dtype=jnp.int32)
    k_idx = jnp.arange(k_count, dtype=jnp.int32)
    u_idx = jnp.arange(second, dtype=jnp.int32)
    m_idx = jnp.arange(m_count, dtype=jnp.int32)
    section_re, section_im = phase_table(v_idx, k_idx, first_radix, -1.0)
    part_re, part_im = complex_product("rvu,vk->rku", shaped, None, section_re, section_im)
    twist_re, twist_im = phase_table(k_idx, u_idx, length, -1.0)
    turned_re = part_re * twist_re - part_im * twist_im
    turned_im = part_re * twist_im + part_im * twist_re
    final_re, final_im = phase_table(u_idx, m_idx, second, -1.0)
    done_re, done_im = complex_product("rku,um->rkm", turned_re, turned_im, final_re, final_im)
    return (
        done_re.reshape(row_count, k_count * m_count),
        done_im.reshape(row_count, k_count * m_count),
    )


def rows_inverse(spec_re, spec_im, length, m_count):
    row_count = spec_re.shape[0]
    second = length // first_radix
    shaped_re = spec_re.reshape(row_count, first_radix, m_count)
    shaped_im = spec_im.reshape(row_count, first_radix, m_count)
    k_idx = jnp.arange(first_radix, dtype=jnp.int32)
    u_idx = jnp.arange(second, dtype=jnp.int32)
    m_idx = jnp.arange(m_count, dtype=jnp.int32)
    section_re, section_im = phase_table(m_idx, u_idx, second, 1.0)
    part_re, part_im = complex_product("rkm,mu->rku", shaped_re, shaped_im, section_re, section_im)
    twist_re, twist_im = phase_table(k_idx, u_idx, length, 1.0)
    turned_re = part_re * twist_re - part_im * twist_im
    turned_im = part_re * twist_im + part_im * twist_re
    final_re, final_im = phase_table(k_idx, k_idx, first_radix, 1.0)
    done_re, done_im = complex_product("rku,kv->rvu", turned_re, turned_im, final_re, final_im)
    return (done_re.reshape(row_count, length), done_im.reshape(row_count, length))


def transform_first(real_in, imag_in, orient):
    length, col_count = real_in.shape
    factor_one = first_factor_of(length)
    second = length // factor_one
    shaped_re = real_in.reshape(factor_one, second, col_count)
    shaped_im = imag_in.reshape(factor_one, second, col_count)
    first_idx = jnp.arange(factor_one, dtype=jnp.int32)
    second_idx = jnp.arange(second, dtype=jnp.int32)
    section_re, section_im = phase_table(first_idx, first_idx, factor_one, orient)
    part_re, part_im = complex_product("abc,ak->kbc", shaped_re, shaped_im, section_re, section_im)
    twist_re, twist_im = phase_table(first_idx, second_idx, length, orient)
    twist_re = twist_re[:, :, None]
    twist_im = twist_im[:, :, None]
    turned_re = part_re * twist_re - part_im * twist_im
    turned_im = part_re * twist_im + part_im * twist_re
    final_re, final_im = phase_table(second_idx, second_idx, second, orient)
    done_re, done_im = complex_product("kbc,bm->mkc", turned_re, turned_im, final_re, final_im)
    return (done_re.reshape(length, col_count), done_im.reshape(length, col_count))


def wavenumbers(indices, length):
    signed = jnp.where(indices < length // 2, indices, indices - length)
    return (two_pi / length * signed.astype(jnp.float32), indices != length // 2)


def poisson_kernel(wave_row, retain_row, wave_col, retain_col, norm_factor):
    squared = wave_col * wave_col + wave_row * wave_row
    retain = retain_row & retain_col & (squared > 0.0)
    safe_sq = jnp.where(retain, squared, 1.0)
    return jnp.where(retain, -2.0 / (safe_sq * norm_factor), 0.0)


def half_spectra(
    piece_re, piece_im, wave_row, retain_row, wave_col, retain_col, col_idx, norm_factor
):
    kernel = poisson_kernel(wave_row, retain_row, wave_col, retain_col, norm_factor)
    weight = jnp.where(col_idx == 0, 1.0, 2.0).astype(jnp.float32)
    phi_re = kernel * weight * piece_re
    phi_im = kernel * weight * piece_im
    cross_term = wave_col * wave_row
    col_sq = wave_col * wave_col
    row_sq = wave_row * wave_row
    all_re = [
        -wave_col * phi_im,
        -wave_row * phi_im,
        -col_sq * phi_re,
        -row_sq * phi_re,
        -cross_term * phi_re,
    ]
    all_im = [
        wave_col * phi_re,
        wave_row * phi_re,
        -col_sq * phi_im,
        -row_sq * phi_im,
        -cross_term * phi_im,
    ]
    return (jnp.stack(all_re), jnp.stack(all_im))


def spectral_rows(spec_re, spec_im, col_begin, ray_all, stride, maker, count, m_count):
    length, col_count = spec_re.shape
    block_cols = min(col_count, 256)
    blocks = col_count // block_cols
    freq_idx = jnp.arange(length, dtype=jnp.int32)
    wave_row, retain_row = wavenumbers(freq_idx, length)
    ray_idx = jnp.arange(ray_all, dtype=jnp.int32) * stride
    back_re, back_im = phase_table(ray_idx, freq_idx, length, 1.0)
    norm_factor = float(length * length)

    def one_block(block_index, result):
        offset = block_index * block_cols
        piece_re = lax.dynamic_slice_in_dim(spec_re, offset, block_cols, 1)
        piece_im = lax.dynamic_slice_in_dim(spec_im, offset, block_cols, 1)
        position = col_begin + offset + jnp.arange(block_cols, dtype=jnp.int32)
        col_idx = first_radix * (position % m_count) + position // m_count
        wave_col, retain_col = wavenumbers(col_idx, length)
        packed_re, packed_im = maker(
            piece_re,
            piece_im,
            wave_row[:, None],
            retain_row[:, None],
            wave_col[None, :],
            retain_col[None, :],
            col_idx[None, :],
            norm_factor,
        )
        out_re, out_im = complex_product("fkc,rk->frc", packed_re, packed_im, back_re, back_im)
        return lax.dynamic_update_slice_in_dim(
            result, jnp.stack([out_re, out_im], axis=1), offset, 3
        )

    initial = jnp.zeros((count, 2, ray_all, col_count), jnp.float32)
    return lax.fori_loop(0, blocks, one_block, initial)


def per_device(density, lens_weight, plane_count, ray_state):
    sky_count = lax.axis_size("sky")
    sky_index = lax.axis_index("sky")
    plane_cells = density[0]
    length = plane_cells.shape[1]
    second = length // first_radix
    ray_dev = ray_state.shape[2]
    ray_all = ray_dev * sky_count
    stride = length // ray_all
    strength = lens_weight[0] * plane_count[0].astype(jnp.float32)
    back_count = second // 2
    row_re, row_im = rows_forward(plane_cells, first_radix, back_count)
    spread = lax.all_to_all(
        jnp.stack([row_re, row_im]), "sky", split_axis=2, concat_axis=1, tiled=True
    )
    spec_re, spec_im = transform_first(spread[0], spread[1], -1.0)
    half_count = length // (2 * sky_count)
    packed = spectral_rows(
        spec_re, spec_im, sky_index * half_count, ray_all, stride, half_spectra, 5, back_count
    )
    returned = lax.all_to_all(packed, "sky", split_axis=2, concat_axis=3, tiled=True)
    count = returned.shape[0]
    width_in = returned.shape[3]
    flat_re = returned[:, 0].reshape(count * ray_dev, width_in)
    flat_im = returned[:, 1].reshape(count * ray_dev, width_in)
    field_re, field_im = rows_inverse(flat_re, flat_im, length, back_count)
    fields = field_re.reshape(5, ray_dev, length) * strength
    ray_tile = ray_state
    current = fields
    for step_index in range(HOPS):
        ray_tile = lens_step(ray_tile, current[None])
        if step_index + 1 < HOPS:
            current = shifted(current, "los", -1)
    ray_tile = shifted(ray_tile, "los", HOPS)
    return ray_tile


def solution(mesh):
    return jax.shard_map(
        per_device,
        mesh=mesh,
        in_specs=(
            P(("real", "los"), "sky", None),
            P(("real", "los")),
            P(("real", "los")),
            P(("real", "los"), None, "sky", None),
        ),
        out_specs=P(("real", "los"), None, "sky", None),
        check_vma=False,
    )
```

profile of v0, /device:TPU:0, one launch (start us, length us, event | category | flops | bytes accessed | tf_op | source)
XLA Modules:
  0.0 469.8 jit_solution(12532667981674408315)
XLA Ops:
  5.5 9.5 %fusion.217 = f32[16,1024,128]{2,0,1:T(8,128)} fusion(f32[1024,16,128]{2,1,0:T(8,128)S(1)} %bitcast.186), kind=kOutput, calls=%fused_computation.286 | convolution fusion | flops 402656768 | bytes 16777216 | tf_op jit(solution)/shard_map/rvu,vk->rku/dot_general | solution.py:77
  14.9 13.3 %subtract_bitcast_fusion = (f32[1024,16,128]{2,1,0:T(8,128)S(1)}, f32[1024,16,128]{2,1,0:T(8,128)S(1)}) fusion(f32[16,1024,128]{2,0,1:T(8,128)} %fusion.217, f32[16,128]{1,0:T(8,128)S(1)} %get-tuple-element.456, f32[16,128]{1,0:T(8,128)S(1)} %get-tuple-element.457, f32[1024,16,128]{2,1,0:T(8,128)} %bitcast.187), kind=kOutput, calls=%fused_computation.93 | convolution fusion | flops 415239680 | bytes 33570816 | tf_op jit(solution)/shard_map/rvu,vk->rku/dot_general | solution.py:77
  28.3 12.4 %fusion.71 = f32[1024,16,64]{0,2,1:T(8,128)S(1)} fusion(f32[1024,16,128]{2,1,0:T(8,128)S(1)} %get-tuple-element.442), kind=kOutput, calls=%fused_computation.96 | convolution fusion | flops 1610727424 | bytes 12582912 | tf_op jit(solution)/shard_map/rku,um->rkm/dot_general | solution.py:77
  40.7 14.0 %fusion.69 = f32[1024,16,64]{0,2,1:T(8,128)} fusion(f32[1024,16,128]{2,1,0:T(8,128)S(1)} %get-tuple-element.442), kind=kOutput, calls=%fused_computation.94 | convolution fusion | flops 1610727424 | bytes 12582912 | tf_op jit(solution)/shard_map/rku,um->rkm/dot_general | solution.py:77
  54.7 14.1 %fusion.105 = f32[1024,16,64]{0,2,1:T(8,128)} fusion(f32[1024,16,64]{0,2,1:T(8,128)S(1)} %fusion.71, f32[1024,16,128]{2,1,0:T(8,128)S(1)} %get-tuple-element.441), kind=kOutput, calls=%fused_computation.124 | convolution fusion | flops 1611776000 | bytes 16777216 | tf_op jit(solution)/shard_map/rku,um->rkm/dot_general | solution.py:77
  68.8 8.7 %copy.71 = f32[1,1024,1024]{1,0,2:T(1,128)} copy(f32[1,1024,1024]{1,2,0:T(8,128)} %bitcast.194) | data formatting | bytes 8388608 | tf_op jit(solution)/shard_map/stack;reshape | solution.py:244
  77.5 17.8 %fusion.108 = f32[1024,16,64]{0,2,1:T(8,128)} fusion(f32[1024,16,64]{0,2,1:T(8,128)S(1)} %copy-done.7, f32[1024,16,128]{2,1,0:T(8,128)} %copy-done.2), kind=kOutput, calls=%fused_computation.125 | convolution fusion | flops 1611776000 | bytes 16777216 | tf_op jit(solution)/shard_map/rku,um->rkm/dot_general | solution.py:77
  95.3 8.6 %copy.72 = f32[1,1024,1024]{1,0,2:T(1,128)} copy(f32[1,1024,1024]{1,2,0:T(8,128)} %bitcast.193) | data formatting | bytes 8388608 | tf_op jit(solution)/shard_map/stack;reshape | solution.py:244
  103.9 8.7 %pad_maximum_fusion.1 = f32[2,1024,1024]{1,0,2:T(2,128)S(1)} fusion(f32[1,1024,1024]{1,0,2:T(1,128)} %copy.72, f32[1,1024,1024]{1,0,2:T(1,128)S(1)} %copy-done.8), kind=kLoop, calls=%fused_computation.91 | loop fusion | flops 2097152 | bytes 16777216 | tf_op jit(solution)/shard_map/stack | solution.py:244
  112.6 10.6 %all_to_all.33 = f32[2,1024,1024]{1,0,2:T(2,128)S(1)} all-to-all(f32[2,1024,1024]{1,0,2:T(2,128)S(1)} %pad_maximum_fusion.1), channel_id=1, replica_groups=mesh['real'=2,'los'=8,'sky'=2] {'sky'}, dimensions={2} | all-to-all | bytes 16777216 | tf_op jit(solution)/shard_map/all_to_all | solution.py:243
  135.5 10.3 %fusion.87 = f32[64,32,512]{2,0,1:T(8,128)} fusion(f32[64,32,512]{2,1,0:T(8,128)} %bitcast.190), kind=kOutput, calls=%fused_computation.114 | convolution fusion | flops 805363712 | bytes 8388608 | tf_op jit(solution)/shard_map/abc,ak->kbc/dot_general | solution.py:77
  145.8 7.1 %fusion.85 = f32[64,32,512]{2,0,1:T(8,128)} fusion(f32[64,32,512]{2,1,0:T(8,128)S(1)} %bitcast.191), kind=kOutput, calls=%fused_computation.112 | convolution fusion | flops 805363712 | bytes 8388608 | tf_op jit(solution)/shard_map/abc,ak->kbc/dot_general | solution.py:77
  158.7 9.9 %fusion.93 = f32[64,32,512]{2,0,1:T(8,128)S(1)} fusion(f32[64,32,512]{2,0,1:T(8,128)} %fusion.87, f32[64,32,512]{2,1,0:T(8,128)} %bitcast.188), kind=kOutput, calls=%fused_computation.120 | convolution fusion | flops 806412288 | bytes 12582912 | tf_op jit(solution)/shard_map/abc,ak->kbc/dot_general | solution.py:77
  168.6 7.4 %multiply_subtract_fusion = (f32[64,32,512]{2,0,1:T(8,128)S(1)}, f32[64,32,512]{2,0,1:T(8,128)S(1)}) fusion(f32[64,32,512]{2,0,1:T(8,128)S(1)} %fusion.93, f32[64,32]{0,1:T(8,128)S(1)} %get-tuple-element.458, f32[64,32]{0,1:T(8,128)S(1)} %get-tuple-element.459, f32[64,32,512]{2,0,1:T(8,128)S(1)} %copy-done.6, f32[64,32,512]{2,1,0:T(8,128)S(1)} %bitcast.189), kind=kOutput, calls=%fused_computation.103 | convolution fusion | flops 812703744 | bytes 20987904 | tf_op jit(solution)/shard_map/abc,ak->kbc/dot_general | solution.py:77
  176.1 5.9 %fusion.77 = f32[32,64,512]{2,0,1:T(8,128)S(1)} fusion(f32[64,32,512]{2,0,1:T(8,128)S(1)} %get-tuple-element.444), kind=kOutput, calls=%fused_computation.104 | convolution fusion | flops 402667520 | bytes 8388608 | tf_op jit(solution)/shard_map/kbc,bm->mkc/dot_general | solution.py:77
  182.0 6.4 %fusion.79 = f32[32,64,512]{2,0,1:T(8,128)S(1)} fusion(f32[64,32,512]{2,0,1:T(8,128)S(1)} %get-tuple-element.444), kind=kOutput, calls=%fused_computation.106 | convolution fusion | flops 402667520 | bytes 8388608 | tf_op jit(solution)/shard_map/kbc,bm->mkc/dot_general | solution.py:77
  188.4 6.2 %fusion.102 = f32[32,64,512]{2,0,1:T(8,128)S(1)} fusion(f32[32,64,512]{2,0,1:T(8,128)S(1)} %fusion.77, f32[64,32,512]{2,0,1:T(8,128)S(1)} %get-tuple-element.443), kind=kOutput, calls=%fused_computation.123 | convolution fusion | flops 403716096 | bytes 12582912 | tf_op jit(solution)/shard_map/kbc,bm->mkc/dot_general | solution.py:77
  199.1 6.3 %fusion.99 = f32[32,64,512]{2,0,1:T(8,128)S(1)} fusion(f32[32,64,512]{2,0,1:T(8,128)S(1)} %fusion.79, f32[64,32,512]{2,0,1:T(8,128)S(1)} %get-tuple-element.443), kind=kOutput, calls=%fused_computation.122 | convolution fusion | flops 403716096 | bytes 12582912 | tf_op jit(solution)/shard_map/kbc,bm->mkc/dot_general | solution.py:77
  210.0 121.0 %while.19 = (s32[]{:T(128)}, f32[5,2,32,512]{3,1,0,2:T(2,128)S(1)}, s32[]{:T(128)}, f32[2048,512]{1,0:T(8,128)}, f32[2048,512]{1,0:T(8,128)}, /*index=5*/s32[32]...) while((s32[]{:T(128)}, f32[5,2,32,512]{3,1,0,2:T(2,128)S(1)}, ...), condition=%wide.region_1.2_spmd.clone.clone.clone, body=%wide.region_0.1_spmd.clone.clone.clone.sunk | while | flops 4079728128 | bytes 115730168 | solution.py:228
  249.1 7.2 %fusion.392 = f32[5,256,32]{1,2,0:T(8,128)S(1)} fusion(f32[5,2048,256]{2,1,0:T(8,128)S(1)} %get-tuple-element.513, s32[32]{0:T(128)S(1)} %get-tuple-element.540), kind=kOutput, calls=%fused_computation.43.clone.1 | convolution fusion | flops 1007550464 | bytes 10649728 | tf_op jit(solution)/shard_map/while/body/eval_jaxpr/fkc,rk->frc/dot_general | solution.py:77
  256.3 7.2 %fusion.393 = f32[5,1,32,256]{3,2,0,1:T(8,128)S(1)} fusion(f32[5,256,32]{1,2,0:T(8,128)S(1)} %fusion.392, f32[5,2048,256]{2,1,0:T(8,128)S(1)} %bitcast_dynamic-update-slice_fusion.25, s32[32]{0:T(128)S(1)} %get-tuple-element.540), kind=kOutput, calls=%fused_computation.30.clone.1 | convolution fusion | flops 1007591424 | bytes 10813568 | tf_op jit(solution)/shard_map/while/body/eval_jaxpr/fkc,rk->frc/dot_general | solution.py:77
  263.5 7.2 %fusion.390 = f32[5,256,32]{1,2,0:T(8,128)S(1)} fusion(f32[5,2048,256]{2,1,0:T(8,128)S(1)} %get-tuple-element.513, s32[32]{0:T(128)S(1)} %get-tuple-element.540), kind=kOutput, calls=%fused_computation.39.clone.1 | convolution fusion | flops 1007550464 | bytes 10649728 | tf_op jit(solution)/shard_map/while/body/eval_jaxpr/fkc,rk->frc/dot_general | solution.py:77
  270.7 7.2 %fusion.391 = f32[5,1,32,256]{3,2,0,1:T(8,128)S(1)} fusion(f32[5,256,32]{1,2,0:T(8,128)S(1)} %fusion.390, f32[5,2048,256]{2,1,0:T(8,128)S(1)} %bitcast_dynamic-update-slice_fusion.25, s32[32]{0:T(128)S(1)} %get-tuple-element.540), kind=kOutput, calls=%fused_computation.28.clone.1 | convolution fusion | flops 1007591424 | bytes 10813568 | tf_op jit(solution)/shard_map/while/body/eval_jaxpr/fkc,rk->frc/dot_general | solution.py:77
  295.7 7.2 %fusion.392 = f32[5,256,32]{1,2,0:T(8,128)S(1)} fusion(f32[5,2048,256]{2,1,0:T(8,128)S(1)} %get-tuple-element.513, s32[32]{0:T(128)S(1)} %get-tuple-element.540), kind=kOutput, calls=%fused_computation.43.clone.1 | convolution fusion | flops 1007550464 | bytes 10649728 | tf_op jit(solution)/shard_map/while/body/eval_jaxpr/fkc,rk->frc/dot_general | solution.py:77
  302.9 7.2 %fusion.393 = f32[5,1,32,256]{3,2,0,1:T(8,128)S(1)} fusion(f32[5,256,32]{1,2,0:T(8,128)S(1)} %fusion.392, f32[5,2048,256]{2,1,0:T(8,128)S(1)} %bitcast_dynamic-update-slice_fusion.25, s32[32]{0:T(128)S(1)} %get-tuple-element.540), kind=kOutput, calls=%fused_computation.30.clone.1 | convolution fusion | flops 1007591424 | bytes 10813568 | tf_op jit(solution)/shard_map/while/body/eval_jaxpr/fkc,rk->frc/dot_general | solution.py:77
  310.1 7.2 %fusion.390 = f32[5,256,32]{1,2,0:T(8,128)S(1)} fusion(f32[5,2048,256]{2,1,0:T(8,128)S(1)} %get-tuple-element.513, s32[32]{0:T(128)S(1)} %get-tuple-element.540), kind=kOutput, calls=%fused_computation.39.clone.1 | convolution fusion | flops 1007550464 | bytes 10649728 | tf_op jit(solution)/shard_map/while/body/eval_jaxpr/fkc,rk->frc/dot_general | solution.py:77
  317.3 7.2 %fusion.391 = f32[5,1,32,256]{3,2,0,1:T(8,128)S(1)} fusion(f32[5,256,32]{1,2,0:T(8,128)S(1)} %fusion.390, f32[5,2048,256]{2,1,0:T(8,128)S(1)} %bitcast_dynamic-update-slice_fusion.25, s32[32]{0:T(128)S(1)} %get-tuple-element.540), kind=kOutput, calls=%fused_computation.28.clone.1 | convolution fusion | flops 1007591424 | bytes 10813568 | tf_op jit(solution)/shard_map/while/body/eval_jaxpr/fkc,rk->frc/dot_general | solution.py:77
  343.7 6.0 %collective-permute-start = (f32[5,16,2048]{2,1,0:T(8,128)}, f32[5,16,2048]{2,1,0:T(8,128)S(1)}, u32[]{:S(2)}, u32[]{:S(2)}) collective-permute-start(f32[5,16,2048]{2,1,0:T(8,128)} %mul.1716), channel_id=1, source_target_pairs={{2,0},{4,2},{6,4},{8,6},{10,8},{12,10},{14,12},{0,14},{3,1},{5,3},... | collective-permute-start | bytes 1966088 | tf_op jit(solution)/shard_map/ppermute | solution.py:16
  349.8 14.5 %collective-permute-done = f32[5,16,2048]{2,1,0:T(8,128)S(1)} collective-permute-done((f32[5,16,2048]{2,1,0:T(8,128)}, f32[5,16,2048]{2,1,0:T(8,128)S(1)}, u32[]{:S(2)}, u32[]{:S(2)}) %collective-permute-start) | collective-permute-done | bytes 655392 | tf_op jit(solution)/shard_map/ppermute | solution.py:16
  369.6 13.2 %collective-permute-done.1 = f32[5,16,2048]{2,1,0:T(8,128)S(1)} collective-permute-done((f32[5,16,2048]{2,1,0:T(8,128)S(1)}, f32[5,16,2048]{2,1,0:T(8,128)S(1)}, u32[]{:S(2)}, u32[]{:S(2)}) %collective-permute-start.1) | collective-permute-done | bytes 655392 | tf_op jit(solution)/shard_map/ppermute | solution.py:16
  388.2 13.9 %collective-permute-done.2 = f32[5,16,2048]{2,1,0:T(8,128)S(1)} collective-permute-done((f32[5,16,2048]{2,1,0:T(8,128)S(1)}, f32[5,16,2048]{2,1,0:T(8,128)S(1)}, u32[]{:S(2)}, u32[]{:S(2)}) %collective-permute-start.2) | collective-permute-done | bytes 655392 | tf_op jit(solution)/shard_map/ppermute | solution.py:16
  402.7 65.7 %collective-permute-done.3 = f32[1,12,16,2048]{3,2,1,0:T(8,128)S(1)} collective-permute-done((f32[1,12,16,2048]{3,2,1,0:T(8,128)S(1)}, f32[1,12,16,2048]{3,2,1,0:T(8,128)S(1)}, u32[]{:S(2)}, u32[]{:S(2)}) %collective-permute-start.3) | collective-permute-done | bytes 1572896 | tf_op jit(solution)/shard_map/ppermute | solution.py:16
  (108 shorter events, 91.4 us)
Async XLA Ops:
  5.5 9.5 %copy-start.3 = (f32[128,8,16,128]{3,2,1,0:T(8,128)}, f32[128,8,16,128]{3,2,1,0:T(8,128)S(1)}, u32[]{:S(2)}) copy-start(f32[128,8,16,128]{3,2,1,0:T(8,128)S(1)} %copy.90) | copy-start | bytes 25165828
  28.3 26.4 %copy-start.2 = (f32[1024,16,128]{2,1,0:T(8,128)}, f32[1024,16,128]{2,1,0:T(8,128)S(1)}, u32[]{:S(2)}) copy-start(f32[1024,16,128]{2,1,0:T(8,128)S(1)} %get-tuple-element.441) | copy-start | bytes 25165828
  68.8 8.7 %copy-start.7 = (f32[1024,16,64]{0,2,1:T(8,128)S(1)}, f32[1024,16,64]{0,2,1:T(8,128)}, u32[]{:S(2)}) copy-start(f32[1024,16,64]{0,2,1:T(8,128)} %fusion.69) | copy-start | bytes 12582916
  95.3 8.6 %copy-start.8 = (f32[1,1024,1024]{1,0,2:T(1,128)S(1)}, f32[1,1024,1024]{1,0,2:T(1,128)}, u32[]{:S(2)}) copy-start(f32[1,1024,1024]{1,0,2:T(1,128)} %copy.71) | copy-start | bytes 12582916
  135.5 10.3 %copy-start.5 = (f32[1,2,1024,512]{3,2,1,0:T(8,128)S(1)}, f32[1,2,1024,512]{3,2,1,0:T(8,128)}, u32[]{:S(2)}) copy-start(f32[1,2,1024,512]{3,2,1,0:T(8,128)} %copy.76) | copy-start | bytes 12582916
  158.7 9.9 %copy-start.4 = (f32[1,2,1024,512]{3,2,1,0:T(8,128)S(1)}, f32[1,2,1024,512]{3,2,1,0:T(8,128)}, u32[]{:S(2)}) copy-start(f32[1,2,1024,512]{3,2,1,0:T(8,128)} %copy.74) | copy-start | bytes 12582916
  158.7 9.9 %copy-start.6 = (f32[64,32,512]{2,0,1:T(8,128)S(1)}, f32[64,32,512]{2,0,1:T(8,128)}, u32[]{:S(2)}) copy-start(f32[64,32,512]{2,0,1:T(8,128)} %fusion.85) | copy-start | bytes 12582916
  232.0 3.5 copy-start
  235.5 2.2 copy-start.1
  278.4 3.5 copy-start
  281.9 2.2 copy-start.1
  342.0 27.4 %copy-start.9 = (f32[1,12,16,2048]{3,2,1,0:T(8,128)S(1)}, f32[1,12,16,2048]{3,2,1,0:T(8,128)}, u32[]{:S(2)}) copy-start(f32[1,12,16,2048]{3,2,1,0:T(8,128)} %param.9) | copy-start | bytes 4718596
  343.7 20.6 %collective-permute-start = (f32[5,16,2048]{2,1,0:T(8,128)}, f32[5,16,2048]{2,1,0:T(8,128)S(1)}, u32[]{:S(2)}, u32[]{:S(2)}) collective-permute-start(f32[5,16,2048]{2,1,0:T(8,128)} %mul.1716), channel_id=1, source_target_pairs={{2,0},{4,2},{6,4},{8,6},{10,8},{12,10},{14,12},{0,14},{3,1},{5,3},... | collective-permute-start | bytes 1966088 | tf_op jit(solution)/shard_map/ppermute | solution.py:16
  364.3 18.5 %collective-permute-start.1 = (f32[5,16,2048]{2,1,0:T(8,128)S(1)}, f32[5,16,2048]{2,1,0:T(8,128)S(1)}, u32[]{:S(2)}, u32[]{:S(2)}) collective-permute-start(f32[5,16,2048]{2,1,0:T(8,128)S(1)} %collective-permute-done), channel_id=1, source_target_pairs={{2,0},{4,2},{6,4},{8,6},{10,8},{12,10},{14,12},{0,14},{3,1},{5,3},... | collective-permute-start | bytes 1966088 | tf_op jit(solution)/shard_map/ppermute | solution.py:16
  382.9 19.3 %collective-permute-start.2 = (f32[5,16,2048]{2,1,0:T(8,128)S(1)}, f32[5,16,2048]{2,1,0:T(8,128)S(1)}, u32[]{:S(2)}, u32[]{:S(2)}) collective-permute-start(f32[5,16,2048]{2,1,0:T(8,128)S(1)} %collective-permute-done.1), channel_id=1, source_target_pairs={{2,0},{4,2},{6,4},{8,6},{10,8},{12,10},{14,12},{0,14},{3,1},{5,3},... | collective-permute-start | bytes 1966088 | tf_op jit(solution)/shard_map/ppermute | solution.py:16
  402.6 65.8 %collective-permute-start.3 = (f32[1,12,16,2048]{3,2,1,0:T(8,128)S(1)}, f32[1,12,16,2048]{3,2,1,0:T(8,128)S(1)}, u32[]{:S(2)}, u32[]{:S(2)}) collective-permute-start(f32[1,12,16,2048]{3,2,1,0:T(8,128)S(1)} %constant_dynamic-update-slice_fusion), channel_id=1, source_target_pairs={{8,0},{10,2},{12,4},{14,6},{0,8},{2,10},{4,12},{6,14},{9,1},{11,3}... | collective-permute-start | bytes 4718600 | tf_op jit(solution)/shard_map/ppermute | solution.py:16
where the time goes:
time: 478 us; the launch traced here: 470 us
  matrix products  203 us (42%)
  waiting for transfers between devices  107 us (22%)
  local copies, waits for them, and re-layouts  54.4 us (11%)
  other arithmetic  43.8 us (9%)
  loops' own time  28.4 us (6%)
  starting transfers between devices  16.3 us (3%)
  blocking collectives  14.9 us (3%)
    dot_general x28, matrix products, mixed(): jnp.einsum(form, left_op, right_op, precision=highest, preferred_element_...  203 us
    ppermute x4, waiting for transfers between devices, shifted(): return lax.ppermute(block, axis, route)  107 us
    while x14, other arithmetic  29.8 us
    another operation x1, loops' own time, spectral_rows(): return lax.fori_loop(0, blocks, one_block, initial)  28.4 us
    another operation x2, local copies, waits for them, and re-layouts, per_device(): jnp.stack([row_re, row_im])  17.3 us
    ppermute x4, starting transfers between devices, shifted(): return lax.ppermute(block, axis, route)  16.3 us
    slice x3, local copies, waits for them, and re-layouts, per_device(): spec_re, spec_im = transform_first(spread[0], spread[1], -1.0)  15.3 us
    all_to_all x1, blocking collectives, per_device(): lax.all_to_all(jnp.stack([row_re, row_im]), 'sky', split_axis=2, concat_a...  10.6 us
  transfers between devices with their start and end apart: 4, of which 4 were waited for; matrix products, arithmetic and copies ran while one was open for 0% of the time, Pallas kernels for 0%

commit v1 on v0

--- a/solution.py
+++ b/solution.py
@@ -240,8 +240,14 @@
     strength = lens_weight[0] * plane_count[0].astype(jnp.float32)
     back_count = second // 2
     row_re, row_im = rows_forward(plane_cells, first_radix, back_count)
-    spread = lax.all_to_all(
-        jnp.stack([row_re, row_im]), "sky", split_axis=2, concat_axis=1, tiled=True
+    spread = jnp.concatenate(
+        lax.all_to_all(
+            jnp.stack(jnp.split(jnp.stack([row_re, row_im]), lax.axis_size("sky"), axis=2)),
+            "sky",
+            0,
+            0,
+        ),
+        axis=1,
     )
     spec_re, spec_im = transform_first(spread[0], spread[1], -1.0)
     half_count = length // (2 * sky_count)

time: 478 us -> 450 us (0.941)
  local copies, waits for them, and re-layouts: 54.4 us -> 35 us
  matrix products: 203 us -> 196 us
    slice x3 -> x1, local copies, waits for them, and re-layouts: 15.3 us -> 0.98 us  [per_device(): spec_re, spec_im = transform_first(spread[0], spread[1], -1.0)]
    dot_general x28, matrix products: 203 us -> 196 us  [mixed(): jnp.einsum(form, left_op, right_op, precision=highest, preferred_element_...]
    another operation x2, local copies, waits for them, and re-layouts: 17.3 us -> 10.9 us  [per_device(): jnp.stack([row_re, row_im])]
where the time goes in v1:
time: 450 us; the launch traced here: 442 us
  matrix products  196 us (44%)
  waiting for transfers between devices  107 us (24%)
  other arithmetic  41.5 us (9%)
  local copies, waits for them, and re-layouts  35 us (8%)
  loops' own time  28.3 us (6%)
  starting transfers between devices  16.3 us (4%)
  blocking collectives  16.1 us (4%)
    dot_general x28, matrix products, mixed(): jnp.einsum(form, left_op, right_op, precision=highest, preferred_element_...  196 us
    ppermute x4, waiting for transfers between devices, shifted(): return lax.ppermute(block, axis, route)  107 us
    while x14, other arithmetic  31.4 us
    another operation x1, loops' own time, spectral_rows(): return lax.fori_loop(0, blocks, one_block, initial)  28.3 us
    ppermute x4, starting transfers between devices, shifted(): return lax.ppermute(block, axis, route)  16.3 us
    all_to_all x1, blocking collectives, per_device(): lax.all_to_all(jnp.stack(jnp.split(jnp.stack([row_re, row_im]), lax.axis_...  11.8 us
    another operation x2, local copies, waits for them, and re-layouts, per_device(): jnp.stack([row_re, row_im])  10.9 us
  transfers between devices with their start and end apart: 4, of which 4 were waited for; matrix products, arithmetic and copies ran while one was open for 0% of the time, Pallas kernels for 0%

profile of v1, /device:TPU:0, one launch (start us, length us, event | category | flops | bytes accessed | tf_op | source)
XLA Modules:
  0.0 441.9 jit_solution(5276548206694269788)
XLA Ops:
  0.1 5.4 %copy.72 = f32[128,8,16,128]{3,2,1,0:T(8,128)S(1)} copy(f32[128,8,16,128]{3,1,2,0:T(8,128)} %bitcast.207) | data formatting | bytes 16777216
  5.5 9.5 %fusion.220 = f32[16,1024,128]{2,0,1:T(8,128)} fusion(f32[1024,16,128]{2,1,0:T(8,128)S(1)} %bitcast.190), kind=kOutput, calls=%fused_computation.293 | convolution fusion | flops 402656768 | bytes 16777216 | tf_op jit(solution)/shard_map/rvu,vk->rku/dot_general | solution.py:77
  14.9 13.3 %subtract_bitcast_fusion = (f32[1024,16,128]{2,1,0:T(8,128)S(1)}, f32[1024,16,128]{2,1,0:T(8,128)S(1)}) fusion(f32[16,1024,128]{2,0,1:T(8,128)} %fusion.220, f32[16,128]{1,0:T(8,128)S(1)} %get-tuple-element.458, f32[16,128]{1,0:T(8,128)S(1)} %get-tuple-element.459, f32[1024,16,128]{2,1,0:T(8,128)} %bitcast.191), kind=kOutput, calls=%fused_computation.96 | convolution fusion | flops 415239680 | bytes 33570816 | tf_op jit(solution)/shard_map/rvu,vk->rku/dot_general | solution.py:77
  28.3 12.4 %fusion.69 = f32[1024,16,64]{0,2,1:T(8,128)S(1)} fusion(f32[1024,16,128]{2,1,0:T(8,128)S(1)} %get-tuple-element.442), kind=kOutput, calls=%fused_computation.97 | convolution fusion | flops 1610727424 | bytes 12582912 | tf_op jit(solution)/shard_map/rku,um->rkm/dot_general | solution.py:77
  40.7 14.1 %fusion.71 = f32[1024,16,64]{0,2,1:T(8,128)} fusion(f32[1024,16,128]{2,1,0:T(8,128)S(1)} %get-tuple-element.442), kind=kOutput, calls=%fused_computation.99 | convolution fusion | flops 1610727424 | bytes 12582912 | tf_op jit(solution)/shard_map/rku,um->rkm/dot_general | solution.py:77
  54.8 14.0 %fusion.111 = f32[1024,16,64]{0,2,1:T(8,128)} fusion(f32[1024,16,64]{0,2,1:T(8,128)S(1)} %fusion.69, f32[1024,16,128]{2,1,0:T(8,128)S(1)} %get-tuple-element.441), kind=kOutput, calls=%fused_computation.132 | convolution fusion | flops 1611776000 | bytes 16777216 | tf_op jit(solution)/shard_map/rku,um->rkm/dot_general | solution.py:77
  68.8 5.6 %copy.56 = f32[1,1024,1024]{2,1,0:T(8,128)} copy(f32[1,1024,1024]{1,2,0:T(8,128)} %bitcast.198) | data formatting | bytes 8388608 | tf_op jit(solution)/shard_map/stack;reshape | solution.py:245
  74.3 18.5 %fusion.108 = f32[1024,16,64]{0,2,1:T(8,128)} fusion(f32[1024,16,64]{0,2,1:T(8,128)} %fusion.71, f32[1024,16,128]{2,1,0:T(8,128)} %copy-done.2), kind=kOutput, calls=%fused_computation.131 | convolution fusion | flops 1611776000 | bytes 16777216 | tf_op jit(solution)/shard_map/rku,um->rkm/dot_general | solution.py:77
  92.8 5.3 %copy.55 = f32[1,1024,1024]{2,1,0:T(8,128)} copy(f32[1,1024,1024]{1,2,0:T(8,128)} %bitcast.197) | data formatting | bytes 8388608 | tf_op jit(solution)/shard_map/stack;reshape | solution.py:245
  103.0 11.8 %all_to_all.23 = f32[2,2,1024,512]{3,2,1,0:T(8,128)} all-to-all(f32[2,2,1024,512]{3,2,1,0:T(8,128)S(1)} %pad_maximum_fusion.1), channel_id=1, replica_groups=mesh['real'=2,'los'=8,'sky'=2] {'sky'}, dimensions={0} | all-to-all | bytes 16777216 | tf_op jit(solution)/shard_map/all_to_all | solution.py:244
  120.2 6.0 %fusion.90 = f32[64,32,512]{2,0,1:T(8,128)S(1)} fusion(f32[64,32,512]{2,1,0:T(8,128)S(1)} %bitcast.194), kind=kOutput, calls=%fused_computation.121 | convolution fusion | flops 805363712 | bytes 8388608 | tf_op jit(solution)/shard_map/abc,ak->kbc/dot_general | solution.py:77
  126.3 6.5 %fusion.88 = f32[64,32,512]{2,0,1:T(8,128)S(1)} fusion(f32[64,32,512]{2,1,0:T(8,128)S(1)} %bitcast.195), kind=kOutput, calls=%fused_computation.119 | convolution fusion | flops 805363712 | bytes 8388608 | tf_op jit(solution)/shard_map/abc,ak->kbc/dot_general | solution.py:77
  132.9 6.5 %fusion.96 = f32[64,32,512]{2,0,1:T(8,128)S(1)} fusion(f32[64,32,512]{2,0,1:T(8,128)S(1)} %fusion.90, f32[64,32,512]{2,1,0:T(8,128)S(1)} %bitcast.192), kind=kOutput, calls=%fused_computation.127 | convolution fusion | flops 806412288 | bytes 12582912 | tf_op jit(solution)/shard_map/abc,ak->kbc/dot_general | solution.py:77
  139.4 7.5 %multiply_subtract_fusion = (f32[64,32,512]{2,0,1:T(8,128)S(1)}, f32[64,32,512]{2,0,1:T(8,128)S(1)}) fusion(f32[64,32,512]{2,0,1:T(8,128)S(1)} %fusion.96, f32[64,32]{0,1:T(8,128)S(1)} %get-tuple-element.460, f32[64,32]{0,1:T(8,128)S(1)} %get-tuple-element.461, f32[64,32,512]{2,0,1:T(8,128)S(1)} %fusion.88, f32[64,32,512]{2,1,0:T(8,128)S(1)} %bitcast.193), kind=kOutput, calls=%fused_computation.110 | convolution fusion | flops 812703744 | bytes 20987904 | tf_op jit(solution)/shard_map/abc,ak->kbc/dot_general | solution.py:77
  146.9 6.2 %fusion.80 = f32[32,64,512]{2,0,1:T(8,128)S(1)} fusion(f32[64,32,512]{2,0,1:T(8,128)S(1)} %get-tuple-element.444), kind=kOutput, calls=%fused_computation.111 | convolution fusion | flops 402667520 | bytes 8388608 | tf_op jit(solution)/shard_map/kbc,bm->mkc/dot_general | solution.py:77
  153.1 6.3 %fusion.82 = f32[32,64,512]{2,0,1:T(8,128)S(1)} fusion(f32[64,32,512]{2,0,1:T(8,128)S(1)} %get-tuple-element.444), kind=kOutput, calls=%fused_computation.113 | convolution fusion | flops 402667520 | bytes 8388608 | tf_op jit(solution)/shard_map/kbc,bm->mkc/dot_general | solution.py:77
  159.4 6.2 %fusion.105 = f32[32,64,512]{2,0,1:T(8,128)S(1)} fusion(f32[32,64,512]{2,0,1:T(8,128)S(1)} %fusion.80, f32[64,32,512]{2,0,1:T(8,128)S(1)} %get-tuple-element.443), kind=kOutput, calls=%fused_computation.130 | convolution fusion | flops 403716096 | bytes 12582912 | tf_op jit(solution)/shard_map/kbc,bm->mkc/dot_general | solution.py:77
  170.1 6.4 %fusion.102 = f32[32,64,512]{2,0,1:T(8,128)S(1)} fusion(f32[32,64,512]{2,0,1:T(8,128)S(1)} %fusion.82, f32[64,32,512]{2,0,1:T(8,128)S(1)} %get-tuple-element.443), kind=kOutput, calls=%fused_computation.129 | convolution fusion | flops 403716096 | bytes 12582912 | tf_op jit(solution)/shard_map/kbc,bm->mkc/dot_general | solution.py:77
  181.1 122.0 %while.19 = (s32[]{:T(128)}, f32[5,2,32,512]{3,1,0,2:T(2,128)S(1)}, s32[]{:T(128)}, f32[2048,512]{1,0:T(8,128)}, f32[2048,512]{1,0:T(8,128)}, /*index=5*/s32[32]...) while((s32[]{:T(128)}, f32[5,2,32,512]{3,1,0,2:T(2,128)S(1)}, ...), condition=%wide.region_1.2_spmd.clone.clone.clone, body=%wide.region_0.1_spmd.clone.clone.clone.sunk | while | flops 4079728128 | bytes 115730168 | solution.py:228
  220.7 7.2 %fusion.395 = f32[5,256,32]{1,2,0:T(8,128)S(1)} fusion(f32[5,2048,256]{2,1,0:T(8,128)S(1)} %get-tuple-element.515, s32[32]{0:T(128)S(1)} %get-tuple-element.542), kind=kOutput, calls=%fused_computation.43.clone.1 | convolution fusion | flops 1007550464 | bytes 10649728 | tf_op jit(solution)/shard_map/while/body/eval_jaxpr/fkc,rk->frc/dot_general | solution.py:77
  227.9 7.2 %fusion.396 = f32[5,1,32,256]{3,2,0,1:T(8,128)S(1)} fusion(f32[5,256,32]{1,2,0:T(8,128)S(1)} %fusion.395, f32[5,2048,256]{2,1,0:T(8,128)S(1)} %bitcast_dynamic-update-slice_fusion.25, s32[32]{0:T(128)S(1)} %get-tuple-element.542), kind=kOutput, calls=%fused_computation.30.clone.1 | convolution fusion | flops 1007591424 | bytes 10813568 | tf_op jit(solution)/shard_map/while/body/eval_jaxpr/fkc,rk->frc/dot_general | solution.py:77
  235.1 7.2 %fusion.393 = f32[5,256,32]{1,2,0:T(8,128)S(1)} fusion(f32[5,2048,256]{2,1,0:T(8,128)S(1)} %get-tuple-element.515, s32[32]{0:T(128)S(1)} %get-tuple-element.542), kind=kOutput, calls=%fused_computation.39.clone.1 | convolution fusion | flops 1007550464 | bytes 10649728 | tf_op jit(solution)/shard_map/while/body/eval_jaxpr/fkc,rk->frc/dot_general | solution.py:77
  242.3 7.2 %fusion.394 = f32[5,1,32,256]{3,2,0,1:T(8,128)S(1)} fusion(f32[5,256,32]{1,2,0:T(8,128)S(1)} %fusion.393, f32[5,2048,256]{2,1,0:T(8,128)S(1)} %bitcast_dynamic-update-slice_fusion.25, s32[32]{0:T(128)S(1)} %get-tuple-element.542), kind=kOutput, calls=%fused_computation.28.clone.1 | convolution fusion | flops 1007591424 | bytes 10813568 | tf_op jit(solution)/shard_map/while/body/eval_jaxpr/fkc,rk->frc/dot_general | solution.py:77
  267.9 7.2 %fusion.395 = f32[5,256,32]{1,2,0:T(8,128)S(1)} fusion(f32[5,2048,256]{2,1,0:T(8,128)S(1)} %get-tuple-element.515, s32[32]{0:T(128)S(1)} %get-tuple-element.542), kind=kOutput, calls=%fused_computation.43.clone.1 | convolution fusion | flops 1007550464 | bytes 10649728 | tf_op jit(solution)/shard_map/while/body/eval_jaxpr/fkc,rk->frc/dot_general | solution.py:77
  275.1 7.2 %fusion.396 = f32[5,1,32,256]{3,2,0,1:T(8,128)S(1)} fusion(f32[5,256,32]{1,2,0:T(8,128)S(1)} %fusion.395, f32[5,2048,256]{2,1,0:T(8,128)S(1)} %bitcast_dynamic-update-slice_fusion.25, s32[32]{0:T(128)S(1)} %get-tuple-element.542), kind=kOutput, calls=%fused_computation.30.clone.1 | convolution fusion | flops 1007591424 | bytes 10813568 | tf_op jit(solution)/shard_map/while/body/eval_jaxpr/fkc,rk->frc/dot_general | solution.py:77
  282.3 7.2 %fusion.393 = f32[5,256,32]{1,2,0:T(8,128)S(1)} fusion(f32[5,2048,256]{2,1,0:T(8,128)S(1)} %get-tuple-element.515, s32[32]{0:T(128)S(1)} %get-tuple-element.542), kind=kOutput, calls=%fused_computation.39.clone.1 | convolution fusion | flops 1007550464 | bytes 10649728 | tf_op jit(solution)/shard_map/while/body/eval_jaxpr/fkc,rk->frc/dot_general | solution.py:77
  289.5 7.2 %fusion.394 = f32[5,1,32,256]{3,2,0,1:T(8,128)S(1)} fusion(f32[5,256,32]{1,2,0:T(8,128)S(1)} %fusion.393, f32[5,2048,256]{2,1,0:T(8,128)S(1)} %bitcast_dynamic-update-slice_fusion.25, s32[32]{0:T(128)S(1)} %get-tuple-element.542), kind=kOutput, calls=%fused_computation.28.clone.1 | convolution fusion | flops 1007591424 | bytes 10813568 | tf_op jit(solution)/shard_map/while/body/eval_jaxpr/fkc,rk->frc/dot_general | solution.py:77
  315.9 6.0 %collective-permute-start = (f32[5,16,2048]{2,1,0:T(8,128)}, f32[5,16,2048]{2,1,0:T(8,128)S(1)}, u32[]{:S(2)}, u32[]{:S(2)}) collective-permute-start(f32[5,16,2048]{2,1,0:T(8,128)} %mul.1716), channel_id=1, source_target_pairs={{2,0},{4,2},{6,4},{8,6},{10,8},{12,10},{14,12},{0,14},{3,1},{5,3},... | collective-permute-start | bytes 1966088 | tf_op jit(solution)/shard_map/ppermute | solution.py:16
  322.0 14.5 %collective-permute-done = f32[5,16,2048]{2,1,0:T(8,128)S(1)} collective-permute-done((f32[5,16,2048]{2,1,0:T(8,128)}, f32[5,16,2048]{2,1,0:T(8,128)S(1)}, u32[]{:S(2)}, u32[]{:S(2)}) %collective-permute-start) | collective-permute-done | bytes 655392 | tf_op jit(solution)/shard_map/ppermute | solution.py:16
  341.8 13.2 %collective-permute-done.1 = f32[5,16,2048]{2,1,0:T(8,128)S(1)} collective-permute-done((f32[5,16,2048]{2,1,0:T(8,128)S(1)}, f32[5,16,2048]{2,1,0:T(8,128)S(1)}, u32[]{:S(2)}, u32[]{:S(2)}) %collective-permute-start.1) | collective-permute-done | bytes 655392 | tf_op jit(solution)/shard_map/ppermute | solution.py:16
  360.4 13.9 %collective-permute-done.2 = f32[5,16,2048]{2,1,0:T(8,128)S(1)} collective-permute-done((f32[5,16,2048]{2,1,0:T(8,128)S(1)}, f32[5,16,2048]{2,1,0:T(8,128)S(1)}, u32[]{:S(2)}, u32[]{:S(2)}) %collective-permute-start.2) | collective-permute-done | bytes 655392 | tf_op jit(solution)/shard_map/ppermute | solution.py:16
  374.9 65.7 %collective-permute-done.3 = f32[1,12,16,2048]{3,2,1,0:T(8,128)S(1)} collective-permute-done((f32[1,12,16,2048]{3,2,1,0:T(8,128)S(1)}, f32[1,12,16,2048]{3,2,1,0:T(8,128)S(1)}, u32[]{:S(2)}, u32[]{:S(2)}) %collective-permute-start.3) | collective-permute-done | bytes 1572896 | tf_op jit(solution)/shard_map/ppermute | solution.py:16
  (97 shorter events, 79.5 us)
Async XLA Ops:
  5.5 9.5 %copy-start.3 = (f32[128,8,16,128]{3,2,1,0:T(8,128)}, f32[128,8,16,128]{3,2,1,0:T(8,128)S(1)}, u32[]{:S(2)}) copy-start(f32[128,8,16,128]{3,2,1,0:T(8,128)S(1)} %copy.72) | copy-start | bytes 25165828
  28.3 26.5 %copy-start.2 = (f32[1024,16,128]{2,1,0:T(8,128)}, f32[1024,16,128]{2,1,0:T(8,128)S(1)}, u32[]{:S(2)}) copy-start(f32[1024,16,128]{2,1,0:T(8,128)S(1)} %get-tuple-element.441) | copy-start | bytes 25165828
  202.9 4.4 copy-start
  203.0 6.3 %copy-start.1 = (f32[2048,512]{1,0:T(8,128)S(1)}, f32[2048,512]{1,0:T(8,128)}, u32[]{:S(2)}) copy-start(f32[2048,512]{1,0:T(8,128)} %get-tuple-element.541) | copy-start | bytes 12582916 | tf_op jit(solution)/shard_map/while
  249.9 4.4 copy-start
  250.0 6.3 %copy-start.1 = (f32[2048,512]{1,0:T(8,128)S(1)}, f32[2048,512]{1,0:T(8,128)}, u32[]{:S(2)}) copy-start(f32[2048,512]{1,0:T(8,128)} %get-tuple-element.541) | copy-start | bytes 12582916 | tf_op jit(solution)/shard_map/while
  311.4 30.2 %copy-start.4 = (f32[1,12,16,2048]{3,2,1,0:T(8,128)S(1)}, f32[1,12,16,2048]{3,2,1,0:T(8,128)}, u32[]{:S(2)}) copy-start(f32[1,12,16,2048]{3,2,1,0:T(8,128)} %param.9) | copy-start | bytes 4718596
  315.9 20.6 %collective-permute-start = (f32[5,16,2048]{2,1,0:T(8,128)}, f32[5,16,2048]{2,1,0:T(8,128)S(1)}, u32[]{:S(2)}, u32[]{:S(2)}) collective-permute-start(f32[5,16,2048]{2,1,0:T(8,128)} %mul.1716), channel_id=1, source_target_pairs={{2,0},{4,2},{6,4},{8,6},{10,8},{12,10},{14,12},{0,14},{3,1},{5,3},... | collective-permute-start | bytes 1966088 | tf_op jit(solution)/shard_map/ppermute | solution.py:16
  336.5 18.5 %collective-permute-start.1 = (f32[5,16,2048]{2,1,0:T(8,128)S(1)}, f32[5,16,2048]{2,1,0:T(8,128)S(1)}, u32[]{:S(2)}, u32[]{:S(2)}) collective-permute-start(f32[5,16,2048]{2,1,0:T(8,128)S(1)} %collective-permute-done), channel_id=1, source_target_pairs={{2,0},{4,2},{6,4},{8,6},{10,8},{12,10},{14,12},{0,14},{3,1},{5,3},... | collective-permute-start | bytes 1966088 | tf_op jit(solution)/shard_map/ppermute | solution.py:16
  355.0 19.3 %collective-permute-start.2 = (f32[5,16,2048]{2,1,0:T(8,128)S(1)}, f32[5,16,2048]{2,1,0:T(8,128)S(1)}, u32[]{:S(2)}, u32[]{:S(2)}) collective-permute-start(f32[5,16,2048]{2,1,0:T(8,128)S(1)} %collective-permute-done.1), channel_id=1, source_target_pairs={{2,0},{4,2},{6,4},{8,6},{10,8},{12,10},{14,12},{0,14},{3,1},{5,3},... | collective-permute-start | bytes 1966088 | tf_op jit(solution)/shard_map/ppermute | solution.py:16
  374.8 65.8 %collective-permute-start.3 = (f32[1,12,16,2048]{3,2,1,0:T(8,128)S(1)}, f32[1,12,16,2048]{3,2,1,0:T(8,128)S(1)}, u32[]{:S(2)}, u32[]{:S(2)}) collective-permute-start(f32[1,12,16,2048]{3,2,1,0:T(8,128)S(1)} %constant_dynamic-update-slice_fusion), channel_id=1, source_target_pairs={{8,0},{10,2},{12,4},{14,6},{0,8},{2,10},{4,12},{6,14},{9,1},{11,3}... | collective-permute-start | bytes 4718600 | tf_op jit(solution)/shard_map/ppermute | solution.py:16
